TPU v7x, 32 devices: a whole 2x2x4 slice. The times are simulated.
32 devices in a mesh: grp: 2 (over x), row: 16 (over z, y, core).
Axes of the slice: x: 2, y: 2, z: 4, core: 2. Of those that a mesh axis runs over, the one named last changes fastest.
Arguments:
- panels: bfloat16 [3, 8192, 1536], P(None, 'row'), may hold values from -0.099436891 to 0.099436891, as said below
- first_f: bfloat16 [1536, 512], P('row', 'grp'), parts along dimension 1, may hold values from -6 to 6
- first_g: bfloat16 [1536, 512], P('row', 'grp'), parts along dimension 1, may hold values from -6 to 6
- phase: float32 [4, 1536], P('grp'), parts along dimension 0, may hold values from -3.140625 to 3.140625
- wavenum: float32 [4, 1536], P('grp'), parts along dimension 0, may hold values from 0.5 to 2
Outputs:
- final_f: float32 [1536, 512], P('row', 'grp'), parts along dimension 1
- final_g: float32 [1536, 512], P('row', 'grp'), parts along dimension 1
There are 2 independent parts, one for each index of `grp`. A program takes and returns all parts, laid end to end along the dimension named above; an argument that names none is the same for every part. Nothing has to cross between parts.
Inputs may be any that keep to these rules, and one draw needn't show every extreme that they name: `panels`: consecutive sectors' surface functions share part of their shape.
All inputs are finite; a program needn't handle non-finite values.
Results may differ from a plain program's by a relative error of at most 0.013.
Values may be sent and summed in bfloat16 or wider, within the bound.
No kernel may reach another device: no remote copies, remote signals or barrier semaphores. Data moves between devices by JAX's collectives and lax.ppermute only.
A program may use at most 64 MiB of HBM per device.

v0:
```python
import jax
import jax.numpy as jnp
from jax import lax
from jax.sharding import PartitionSpec as P

SECTORS = 2


def contract_rows(left, right):
    return lax.dot_general(
        left, right, (((0,), (0,)), ((), ())), preferred_element_type=jnp.float32
    )


def shards(panels, first_f, first_g, phase, wavenum):
    chan_rows = first_f.shape[0]
    width = first_f.shape[1]
    all_channels = chan_rows * lax.axis_size("row")
    first_row = lax.axis_index("row") * chan_rows
    state = jnp.concatenate([first_f, first_g], axis=1).astype(jnp.float32)
    for sector in range(SECTORS):
        current = panels[sector]
        following = panels[sector + 1]
        solutions = state.astype(jnp.bfloat16)
        flipped = lax.psum_scatter(
            contract_rows(following, current), "row", scatter_dimension=0, tiled=True
        ).astype(jnp.bfloat16)
        rotated = jnp.dot(
            flipped,
            lax.all_gather(solutions, "row", axis=0, tiled=True),
            preferred_element_type=jnp.float32,
        )
        rot_amp = rotated[:, :width]
        rot_der = rotated[:, width:]
        angle_rows = lax.dynamic_slice_in_dim(phase[sector], first_row, chan_rows, 0)
        wave_rows = lax.dynamic_slice_in_dim(wavenum[sector], first_row, chan_rows, 0)
        cosine = jnp.cos(angle_rows)[:, None]
        sine = jnp.sin(angle_rows)[:, None]
        wave = wave_rows[:, None]
        new_amp = cosine * rot_amp + sine / wave * rot_der
        new_der = -wave * sine * rot_amp + cosine * rot_der
        local_norm = jnp.sum(new_amp * new_amp, axis=0) + jnp.sum(new_der * new_der, axis=0)
        norm = lax.psum(local_norm, "row")
        scale = 1.0 / jnp.sqrt(norm / (2.0 * all_channels) + 1e-06)
        state = jnp.concatenate([new_amp * scale[None, :], new_der * scale[None, :]], axis=1)
    return (state[:, :width], state[:, width:])


def solution(mesh):
    in_specs = (
        P(None, "row", None),
        P("row", "grp"),
        P("row", "grp"),
        P("grp", None),
        P("grp", None),
    )
    out_specs = (P("row", "grp"), P("row", "grp"))
    return jax.shard_map(shards, mesh=mesh, in_specs=in_specs, out_specs=out_specs, check_vma=False)
```

profile of v0, /device:TPU:0, one launch (start us, length us, event | category | flops | bytes accessed | tf_op | source)
XLA Modules:
  0.0 366.6 jit_solution(17294964851320102471)
XLA Ops:
  7.2 0.0 all-gather.3.cloned.1.call-start
  7.2 1.5 pad_maximum_fusion
  8.7 0.0 all-gather.3.cloned.1.call-update
  8.7 0.0 reduce-scatter.5.cloned.1.call-start
  8.8 8.2 %fusion = f32[1536,1536]{1,0:T(8,128)} fusion(bf16[3,512,1536]{2,1,0:T(8,128)(2,1)} %param.5), kind=kOutput, calls=%fused_computation | convolution fusion | flops 2415919104 | bytes 12582912 | tf_op jit(solution)/shard_map/dot_general | solution.py:10
  16.9 0.0 reduce-scatter.5.cloned.1.call-update
  17.0 0.0 reduce-scatter.3.cloned.1.call-start
  17.0 8.2 %fusion.3 = f32[1536,1536]{1,0:T(8,128)} fusion(bf16[3,512,1536]{2,1,0:T(8,128)(2,1)} %param.5), kind=kOutput, calls=%fused_computation.3 | convolution fusion | flops 2415919104 | bytes 12582912 | tf_op jit(solution)/shard_map/dot_general | solution.py:10
  25.2 0.0 copy-start
  25.2 0.0 copy-start.1
  25.2 0.0 reduce-scatter.3.cloned.1.call-update
  25.2 0.0 all-gather.5.cloned.1.call-start
  25.3 0.6 copy-done
  25.9 0.0 copy-done.1
  25.9 0.1 cosine_bitcast_fusion
  26.0 0.1 bitcast_divide_fusion.1
  26.2 27.1 %all-gather.3.cloned.1.call-done = bf16[1536,512]{1,0:T(8,128)(2,1)} async-done(((bf16[96,512]{1,0:T(8,128)(2,1)}), bf16[1536,512]{1,0:T(8,128)(2,1)}) %all-gather.3.cloned.1.call-update) | async-done | bytes 1572880 | tf_op jit(solution)/shard_map/all_gather | solution.py:30
  53.3 114.4 %reduce-scatter.5.cloned.1.call-done = f32[96,1536]{1,0:T(8,128)} async-done(((f32[1536,1536]{1,0:T(8,128)}), f32[96,1536]{1,0:T(8,128)}) %reduce-scatter.5.cloned.1.call-update) | async-done | bytes 589840 | tf_op jit(solution)/shard_map/reduce_scatter | solution.py:25
  167.6 2.0 fusion.10
  169.6 0.1 multiply_reduce_fusion.2
  169.7 32.2 %psum.14 = f32[256]{0:T(256)S(1)} all-reduce(f32[256]{0:T(256)S(1)} %add.41), channel_id=1, replica_groups=mesh['grp'=2,'row'=16] {'row'}, use_global_device_ids=true, to_apply=%region_4.0 | all-reduce | flops 256 | bytes 2048 | tf_op jit(solution)/shard_map/psum | solution.py:43
  202.0 0.1 multiply_convert_fusion.1
  202.1 0.6 pad_maximum_fusion.1
  202.7 0.0 all-gather.5.cloned.1.call-update
  202.8 0.1 cosine_bitcast_fusion.1
  202.9 0.1 bitcast_divide_fusion
  203.0 80.4 %reduce-scatter.3.cloned.1.call-done = f32[96,1536]{1,0:T(8,128)} async-done(((f32[1536,1536]{1,0:T(8,128)}), f32[96,1536]{1,0:T(8,128)}) %reduce-scatter.3.cloned.1.call-update) | async-done | bytes 589840 | tf_op jit(solution)/shard_map/reduce_scatter | solution.py:25
  283.4 42.2 %all-gather.5.cloned.1.call-done = bf16[1536,512]{1,0:T(8,128)(2,1)} async-done(((bf16[96,512]{1,0:T(8,128)(2,1)}), bf16[1536,512]{1,0:T(8,128)(2,1)}) %all-gather.5.cloned.1.call-update) | async-done | bytes 1572880 | tf_op jit(solution)/shard_map/all_gather | solution.py:30
  325.6 2.0 fusion.12
  327.6 0.1 multiply_reduce_fusion
  327.7 31.6 %psum.15 = f32[256]{0:T(256)S(1)} all-reduce(f32[256]{0:T(256)S(1)} %add.45), channel_id=1, replica_groups=mesh['grp'=2,'row'=16] {'row'}, use_global_device_ids=true, to_apply=%region_7.0 | all-reduce | flops 256 | bytes 2048 | tf_op jit(solution)/shard_map/psum | solution.py:43
  359.3 0.8 broadcast_multiply_fusion
  (5 shorter events, 0.0 us)
Async XLA Ops:
  7.2 46.1 %all-gather.3.cloned.1.call-start = ((), (), s32[]{:S(2)}) async-start(), calls=%async_computation.4 | async-start | bytes 1671168 | tf_op jit(solution)/shard_map/all_gather | solution.py:30
  8.7 158.9 %reduce-scatter.5.cloned.1.call-start = ((), (), s32[]{:S(2)}) async-start(), calls=%async_computation.3 | async-start | bytes 10027008 | tf_op jit(solution)/shard_map/reduce_scatter | solution.py:25
  17.0 266.4 %reduce-scatter.3.cloned.1.call-start = ((), (), s32[]{:S(2)}) async-start(), calls=%async_computation.2 | async-start | bytes 10027008 | tf_op jit(solution)/shard_map/reduce_scatter | solution.py:25
  25.2 0.7 copy-start
  25.2 0.7 copy-start.1
  25.2 300.4 %all-gather.5.cloned.1.call-start = ((), (), s32[]{:S(2)}) async-start(), calls=%async_computation.5 | async-start | bytes 1671168 | tf_op jit(solution)/shard_map/all_gather | solution.py:30
Sparse Core Ops, SparseCore 0:
  10.9 42.3 all-gather.2
  57.4 110.2 reduce-scatter.4
  172.3 111.0 reduce-scatter.2
  286.1 39.4 all-gather.4
where the time goes:
time: 367 us
  waiting for transfers between devices  264 us (72%)
  blocking collectives  63.8 us (17%)
  matrix products  20.3 us (6%)
  between operations  13.8 us (4%)
    reduce_scatter x2, waiting for transfers between devices, shards(): lax.psum_scatter(contract_rows(following, current), 'row', scatter_dimens...  195 us
    all_gather x2, waiting for transfers between devices, shards(): lax.all_gather(solutions, 'row', axis=0, tiled=True)  69.3 us
    psum x2, blocking collectives, shards(): norm = lax.psum(local_norm, 'row')  63.8 us
    dot_general x2, matrix products, contract_rows(): lax.dot_general(left, right, (((0,), (0,)), ((), ())), preferred_element_...  16.3 us
  transfers between devices with their start and end apart: 4, of which 4 were waited for; matrix products, arithmetic and copies ran while one was open for 5% of the time, Pallas kernels for 0%

commit v1 on v0

--- a/solution.py
+++ b/solution.py
@@ -4,6 +4,28 @@
 from jax.sharding import PartitionSpec as P
 
 SECTORS = 2
+
+
+def laid_out(blocks, dim):
+    dims = list(blocks.shape[1:])
+    dims[dim] *= blocks.shape[0]
+    return jnp.moveaxis(blocks, 0, dim).reshape(dims)
+
+
+def grow_blocks(array, axis):
+    count = lax.axis_size(axis)
+    parts = array[None]
+    for level in range(count.bit_length() - 1):
+        bit = 1 << level
+        other = lax.ppermute(parts, axis, [(i, i ^ bit) for i in range(count)])
+        both = jnp.stack([parts, other])
+        upper = lax.axis_index(axis) >> level & 1
+        parts = jnp.where(upper == 0, both, both[::-1]).reshape(-1, *array.shape)
+    return parts
+
+
+def gather_by_bits(shard, axis, dim):
+    return laid_out(grow_blocks(shard, axis), dim)
 
 
 def contract_rows(left, right):
@@ -26,9 +48,7 @@
             contract_rows(following, current), "row", scatter_dimension=0, tiled=True
         ).astype(jnp.bfloat16)
         rotated = jnp.dot(
-            flipped,
-            lax.all_gather(solutions, "row", axis=0, tiled=True),
-            preferred_element_type=jnp.float32,
+            flipped, gather_by_bits(solutions, "row", 0), preferred_element_type=jnp.float32
         )
         rot_amp = rotated[:, :width]
         rot_der = rotated[:, width:]

time: 367 us -> 344 us (0.937)
  waiting for transfers between devices: 264 us -> 233 us
  starting transfers between devices: 0.16 us -> 8.16 us
    ppermute x0 -> x8, waiting for transfers between devices: none -> 168 us  [grow_blocks(): other = lax.ppermute(parts, axis, [(i, i ^ bit) for i in range(count)])]
    reduce_scatter x2, waiting for transfers between devices: 195 us -> 64.6 us  [shards(): lax.psum_scatter(contract_rows(following, current), 'row', scatter_dimens...]
    all_gather x2 -> x0, waiting for transfers between devices: 69.3 us -> none  [shards(): lax.all_gather(solutions, 'row', axis=0, tiled=True)]
    ppermute x0 -> x8, starting transfers between devices: none -> 8.08 us  [grow_blocks(): other = lax.ppermute(parts, axis, [(i, i ^ bit) for i in range(count)])]
  transfers between devices with their start and end apart: 4 -> 10, of which waited for: 4 -> 10; matrix products, arithmetic and copies ran while one was open for 5% -> 4% of each run, Pallas kernels for 0% -> 0%
where the time goes in v1:
time: 344 us; the launch traced here: 343 us
  waiting for transfers between devices  233 us (68%)
  blocking collectives  64.4 us (19%)
  matrix products  19.2 us (6%)
  between operations  14.2 us (4%)
  starting transfers between devices  8.16 us (2%)
    ppermute x8, waiting for transfers between devices, grow_blocks(): other = lax.ppermute(parts, axis, [(i, i ^ bit) for i in range(count)])  168 us
    reduce_scatter x2, waiting for transfers between devices, shards(): lax.psum_scatter(contract_rows(following, current), 'row', scatter_dimens...  64.6 us
    psum x2, blocking collectives, shards(): norm = lax.psum(local_norm, 'row')  64.4 us
    dot_general x2, matrix products, contract_rows(): lax.dot_general(left, right, (((0,), (0,)), ((), ())), preferred_element_...  16.3 us
    ppermute x8, starting transfers between devices, grow_blocks(): other = lax.ppermute(parts, axis, [(i, i ^ bit) for i in range(count)])  8.08 us
  transfers between devices with their start and end apart: 10, of which 10 were waited for; matrix products, arithmetic and copies ran while one was open for 4% of the time, Pallas kernels for 0%

profile of v1, /device:TPU:0, one launch (start us, length us, event | category | flops | bytes accessed | tf_op | source)
XLA Modules:
  0.0 343.3 jit_solution(1641363742500247262)
XLA Ops:
  7.2 8.2 %fusion = f32[1536,1536]{1,0:T(8,128)} fusion(bf16[3,512,1536]{2,1,0:T(8,128)(2,1)} %param.5), kind=kOutput, calls=%fused_computation.4 | convolution fusion | flops 2415919104 | bytes 12582912 | tf_op jit(solution)/shard_map/dot_general | solution.py:32
  15.4 8.2 %fusion.3 = f32[1536,1536]{1,0:T(8,128)} fusion(bf16[3,512,1536]{2,1,0:T(8,128)(2,1)} %param.5), kind=kOutput, calls=%fused_computation.7 | convolution fusion | flops 2415919104 | bytes 12582912 | tf_op jit(solution)/shard_map/dot_general | solution.py:32
  23.6 0.8 copy-done
  24.4 0.5 collective-permute-start
  24.9 1.0 collective-permute-done
  26.1 3.0 collective-permute-start.1
  29.0 5.2 %collective-permute-done.1 = bf16[2,96,512]{2,1,0:T(8,128)(2,1)S(1)} collective-permute-done((bf16[2,96,512]{2,1,0:T(8,128)(2,1)S(1)}, bf16[2,96,512]{2,1,0:T(8,128)(2,1)S(1)}, u32[]{:S(2)}, u32[]{:S(2)}) %collective-permute-start.1) | collective-permute-done | bytes 196640 | tf_op jit(solution)/shard_map/ppermute | solution.py:20
  34.3 1.8 collective-permute-start.2
  36.2 8.9 %collective-permute-done.2 = bf16[4,96,512]{2,1,0:T(8,128)(2,1)S(1)} collective-permute-done((bf16[4,96,512]{2,1,0:T(8,128)(2,1)S(1)}, bf16[4,96,512]{2,1,0:T(8,128)(2,1)S(1)}, u32[]{:S(2)}, u32[]{:S(2)}) %collective-permute-start.2) | collective-permute-done | bytes 393248 | tf_op jit(solution)/shard_map/ppermute | solution.py:20
  45.1 0.2 reverse_select_fusion.3
  45.3 2.5 collective-permute-start.3
  47.9 0.1 bitcast_divide_fusion.1
  48.1 69.3 %collective-permute-done.3 = bf16[8,96,512]{2,1,0:T(8,128)(2,1)S(1)} collective-permute-done((bf16[8,96,512]{2,1,0:T(8,128)(2,1)S(1)}, bf16[8,96,512]{2,1,0:T(8,128)(2,1)S(1)}, u32[]{:S(2)}, u32[]{:S(2)}) %collective-permute-start.3) | collective-permute-done | bytes 786464 | tf_op jit(solution)/shard_map/ppermute | solution.py:20
  117.3 0.1 pad_maximum_fusion
  117.5 0.4 reverse_select_fusion.1
  117.8 43.0 %reduce-scatter.5.cloned.1.call-done = f32[96,1536]{1,0:T(8,128)} async-done(((f32[1536,1536]{1,0:T(8,128)}), f32[96,1536]{1,0:T(8,128)}) %reduce-scatter.5.cloned.1.call-update) | async-done | bytes 589840 | tf_op jit(solution)/shard_map/reduce_scatter | solution.py:47
  160.8 1.4 fusion.10
  162.3 0.1 multiply_reduce_fusion.3
  162.4 32.2 %psum.14 = f32[256]{0:T(256)S(1)} all-reduce(f32[256]{0:T(256)S(1)} %add.41), channel_id=1, replica_groups=mesh['grp'=2,'row'=16] {'row'}, use_global_device_ids=true, to_apply=%region_4.5 | all-reduce | flops 256 | bytes 2048 | tf_op jit(solution)/shard_map/psum | solution.py:63
  194.8 1.3 collective-permute-done.4
  196.2 11.2 %collective-permute-done.5 = bf16[2,96,512]{2,1,0:T(8,128)(2,1)S(1)} collective-permute-done((bf16[2,96,512]{2,1,0:T(8,128)(2,1)S(1)}, bf16[2,96,512]{2,1,0:T(8,128)(2,1)S(1)}, u32[]{:S(2)}, u32[]{:S(2)}) %collective-permute-start.5) | collective-permute-done | bytes 196640 | tf_op jit(solution)/shard_map/ppermute | solution.py:20
  207.5 27.8 %collective-permute-done.6 = bf16[4,96,512]{2,1,0:T(8,128)(2,1)S(1)} collective-permute-done((bf16[4,96,512]{2,1,0:T(8,128)(2,1)S(1)}, bf16[4,96,512]{2,1,0:T(8,128)(2,1)S(1)}, u32[]{:S(2)}, u32[]{:S(2)}) %collective-permute-start.6) | collective-permute-done | bytes 393248 | tf_op jit(solution)/shard_map/ppermute | solution.py:20
  235.4 0.1 reverse_select_fusion.2
  235.7 0.1 bitcast_divide_fusion
  235.9 43.8 %collective-permute-done.7 = bf16[8,96,512]{2,1,0:T(8,128)(2,1)S(1)} collective-permute-done((bf16[8,96,512]{2,1,0:T(8,128)(2,1)S(1)}, bf16[8,96,512]{2,1,0:T(8,128)(2,1)S(1)}, u32[]{:S(2)}, u32[]{:S(2)}) %collective-permute-start.7) | collective-permute-done | bytes 786464 | tf_op jit(solution)/shard_map/ppermute | solution.py:20
  279.7 0.1 pad_maximum_fusion.1
  279.8 0.4 reverse_select_fusion
  280.2 21.6 %reduce-scatter.3.cloned.1.call-done = f32[96,1536]{1,0:T(8,128)} async-done(((f32[1536,1536]{1,0:T(8,128)}), f32[96,1536]{1,0:T(8,128)}) %reduce-scatter.3.cloned.1.call-update) | async-done | bytes 589840 | tf_op jit(solution)/shard_map/reduce_scatter | solution.py:47
  301.8 1.5 fusion.12
  303.3 0.1 multiply_reduce_fusion
  303.4 32.2 %psum.15 = f32[256]{0:T(256)S(1)} all-reduce(f32[256]{0:T(256)S(1)} %add.45), channel_id=1, replica_groups=mesh['grp'=2,'row'=16] {'row'}, use_global_device_ids=true, to_apply=%region_7.8 | all-reduce | flops 256 | bytes 2048 | tf_op jit(solution)/shard_map/psum | solution.py:63
  335.6 0.8 broadcast_multiply_fusion
  (36 shorter events, 1.2 us)
Async XLA Ops:
  7.2 153.7 %reduce-scatter.5.cloned.1.call-start = ((), (), s32[]{:S(2)}) async-start(), calls=%async_computation.3 | async-start | bytes 10027008 | tf_op jit(solution)/shard_map/reduce_scatter | solution.py:47
  15.4 286.4 %reduce-scatter.3.cloned.1.call-start = ((), (), s32[]{:S(2)}) async-start(), calls=%async_computation.2 | async-start | bytes 10027008 | tf_op jit(solution)/shard_map/reduce_scatter | solution.py:47
  23.6 0.8 copy-start
  23.6 0.8 copy-start.1
  24.4 1.5 collective-permute-start
  26.1 8.2 %collective-permute-start.1 = (bf16[2,96,512]{2,1,0:T(8,128)(2,1)S(1)}, bf16[2,96,512]{2,1,0:T(8,128)(2,1)S(1)}, u32[]{:S(2)}, u32[]{:S(2)}) collective-permute-start(bf16[2,96,512]{2,1,0:T(8,128)(2,1)S(1)} %get-tuple-element.15), channel_id=1, source_target_pairs={{0,2},{1,3},{2,0},{3,1},{4,6},{5,7},{6,4},{7,5},{8,10},{9,11},{10,... | collective-permute-start | bytes 589832 | tf_op jit(solution)/shard_map/ppermute | solution.py:20
  34.3 10.7 %collective-permute-start.2 = (bf16[4,96,512]{2,1,0:T(8,128)(2,1)S(1)}, bf16[4,96,512]{2,1,0:T(8,128)(2,1)S(1)}, u32[]{:S(2)}, u32[]{:S(2)}) collective-permute-start(bf16[4,96,512]{2,1,0:T(8,128)(2,1)S(1)} %bitcast.85), channel_id=1, source_target_pairs={{0,4},{1,5},{2,6},{3,7},{4,0},{5,1},{6,2},{7,3},{8,12},{9,13},{10,... | collective-permute-start | bytes 1179656 | tf_op jit(solution)/shard_map/ppermute | solution.py:20
  45.1 2.7 copy-start.2
  45.1 2.7 copy-start.3
  45.3 72.0 %collective-permute-start.3 = (bf16[8,96,512]{2,1,0:T(8,128)(2,1)S(1)}, bf16[8,96,512]{2,1,0:T(8,128)(2,1)S(1)}, u32[]{:S(2)}, u32[]{:S(2)}) collective-permute-start(bf16[8,96,512]{2,1,0:T(8,128)(2,1)S(1)} %bitcast.81), channel_id=1, source_target_pairs={{0,8},{1,9},{2,10},{3,11},{4,12},{5,13},{6,14},{7,15},{8,0},{9,1},... | collective-permute-start | bytes 2359304 | tf_op jit(solution)/shard_map/ppermute | solution.py:20
  194.7 1.4 collective-permute-start.4
  196.1 11.2 %collective-permute-start.5 = (bf16[2,96,512]{2,1,0:T(8,128)(2,1)S(1)}, bf16[2,96,512]{2,1,0:T(8,128)(2,1)S(1)}, u32[]{:S(2)}, u32[]{:S(2)}) collective-permute-start(bf16[2,96,512]{2,1,0:T(8,128)(2,1)S(1)} %get-tuple-element.13), channel_id=1, source_target_pairs={{0,2},{1,3},{2,0},{3,1},{4,6},{5,7},{6,4},{7,5},{8,10},{9,11},{10,... | collective-permute-start | bytes 589832 | tf_op jit(solution)/shard_map/ppermute | solution.py:20
  207.5 27.9 %collective-permute-start.6 = (bf16[4,96,512]{2,1,0:T(8,128)(2,1)S(1)}, bf16[4,96,512]{2,1,0:T(8,128)(2,1)S(1)}, u32[]{:S(2)}, u32[]{:S(2)}) collective-permute-start(bf16[4,96,512]{2,1,0:T(8,128)(2,1)S(1)} %bitcast.87), channel_id=1, source_target_pairs={{0,4},{1,5},{2,6},{3,7},{4,0},{5,1},{6,2},{7,3},{8,12},{9,13},{10,... | collective-permute-start | bytes 1179656 | tf_op jit(solution)/shard_map/ppermute | solution.py:20
  235.5 44.2 %collective-permute-start.7 = (bf16[8,96,512]{2,1,0:T(8,128)(2,1)S(1)}, bf16[8,96,512]{2,1,0:T(8,128)(2,1)S(1)}, u32[]{:S(2)}, u32[]{:S(2)}) collective-permute-start(bf16[8,96,512]{2,1,0:T(8,128)(2,1)S(1)} %bitcast.83), channel_id=1, source_target_pairs={{0,8},{1,9},{2,10},{3,11},{4,12},{5,13},{6,14},{7,15},{8,0},{9,1},... | collective-permute-start | bytes 2359304 | tf_op jit(solution)/shard_map/ppermute | solution.py:20
Sparse Core Ops, SparseCore 0:
  15.5 145.2 reduce-scatter.4
  165.5 136.2 reduce-scatter.2
